TPU v7x, 32 devices: a whole 2x2x4 slice. The times are simulated.
32 devices in a mesh: videos: 2 (over y), ha: 4 (over z), wa: 2 (over x), ta: 2 (over core).
Axes of the slice: x: 2, y: 2, z: 4, core: 2. Of those that a mesh axis runs over, the one named last changes fastest.
Arguments:
- latents: bfloat16 [12, 8, 64, 512], P(('videos', 'ta'), 'ha', 'wa'), parts along dimension 0, may hold values from -200 to 200
- norm1_gain: float32 [512], replicated, may hold values from 0.25 to 1.75
- norm1_shift: float32 [512], replicated, may hold values from -2.5 to 2.5
- up_weight: bfloat16 [3, 3, 512, 256], replicated, may hold values from -0.1875 to 0.1875
- norm2_gain: float32 [256], replicated, may hold values from 0.25 to 1.75
- norm2_shift: float32 [256], replicated, may hold values from -2.5 to 2.5
- conv_a: bfloat16 [3, 3, 3, 256, 256], replicated, may hold values from -0.078125 to 0.078125
- norm3_gain: float32 [256], replicated, may hold values from 0.25 to 1.75
- norm3_shift: float32 [256], replicated, may hold values from -2.5 to 2.5
- conv_b: bfloat16 [3, 3, 3, 256, 256], replicated, may hold values from -0.078125 to 0.078125
Outputs:
- decoded: bfloat16 [12, 16, 128, 256], P(('videos', 'ta'), 'ha', 'wa'), parts along dimension 0
There are 2 independent parts, one for each index of `videos`. A program takes and returns all parts, laid end to end along the dimension named above; an argument that names none is the same for every part. Nothing has to cross between parts.
All inputs are finite; a program needn't handle non-finite values.
Results may differ from a plain program's by a relative error of at most 0.008.
Values may be sent and summed in bfloat16 or wider, within the bound.
No kernel may reach another device: no remote copies, remote signals or barrier semaphores. Data moves between devices by JAX's collectives and lax.ppermute only.
A program may use at most 64 MiB of HBM per device.

v0:
```python
import jax
import jax.numpy as jnp
from jax import lax
from jax.sharding import PartitionSpec as P

GROUPS = 32
EPSILON = 1e-06


def passed_along(block, axis, distance):
    devices = range(lax.axis_size(axis))
    route = [(i - distance, i) for i in devices if i - distance in devices]
    return lax.ppermute(block, axis, route)


def padded_2(x, sides, width):
    for axis, dim in sides:
        size, length = (lax.axis_size(axis), x.shape[dim])
        up = [(i, (i + 1) % size) for i in range(size - 1)]
        down = [(j, i) for i, j in up]
        last = lax.slice_in_dim(x, length - width, length, axis=dim)
        initial = lax.slice_in_dim(x, 0, width, axis=dim)
        before = lax.ppermute(last, axis, up)
        after = lax.ppermute(initial, axis, down)
        x = jnp.concatenate([before, x, after], axis=dim)
    return x


def activate(values, sample, scale_vec, shift_vec):
    channels = values.shape[-1]
    group_width = channels // GROUPS
    grouped = sample.reshape(-1, GROUPS, group_width)
    entries = (
        grouped.shape[0]
        * group_width
        * lax.axis_size("ha")
        * lax.axis_size("wa")
        * lax.axis_size("ta")
    )
    totals, squares = lax.psum(
        (jnp.sum(grouped, axis=(0, 2)), jnp.sum(grouped * grouped, axis=(0, 2))), ("ha", "wa", "ta")
    )
    average = totals / entries
    spread = squares / entries - average * average
    scaling = lax.rsqrt(spread + EPSILON)
    normed = (values - jnp.repeat(average, group_width)) * jnp.repeat(
        scaling, group_width
    ) * scale_vec + shift_vec
    return jax.nn.silu(normed).astype(jnp.bfloat16)


def parity_merge(lead_part, mid_part, tail_part, axis_pos):
    pad_end = [(0, 0)] * lead_part.ndim
    pad_front = [(0, 0)] * lead_part.ndim
    pad_end[axis_pos] = (0, 1)
    pad_front[axis_pos] = (1, 0)
    even_part = jnp.pad(lead_part, pad_end) + jnp.pad(tail_part, pad_front)
    odd_part = jnp.pad(mid_part, pad_end)
    stacked = jnp.stack([even_part, odd_part], axis=axis_pos + 1)
    new_shape = list(even_part.shape)
    new_shape[axis_pos] = new_shape[axis_pos] * 2
    return stacked.reshape(new_shape)


def spread_taps(source, kernel):
    frames, height, across, channels = source.shape
    flattened = source.reshape(-1, channels)
    products = [
        [
            jnp.dot(flattened, kernel[tap_y, tap_x], preferred_element_type=jnp.float32).reshape(
                frames, height, across, -1
            )
            for tap_x in range(3)
        ]
        for tap_y in range(3)
    ]
    columns = [
        parity_merge(products[0][tap_x], products[1][tap_x], products[2][tap_x], 1)
        for tap_x in range(3)
    ]
    return parity_merge(columns[0], columns[1], columns[2], 2)


def valid_conv(padded, kernel, frames, height, across):
    result = jnp.zeros((frames * height * across, kernel.shape[-1]), jnp.float32)
    for step_t in range(3):
        for step_y in range(3):
            for step_x in range(3):
                window = padded[
                    step_t : step_t + frames, step_y : step_y + height, step_x : step_x + across
                ]
                result = result + jnp.dot(
                    window.reshape(-1, window.shape[-1]),
                    kernel[step_t, step_y, step_x],
                    preferred_element_type=jnp.float32,
                )
    return result.reshape(frames, height, across, -1)


def causal_extend(values):
    earlier = passed_along(values[-2:], "ta", 1)
    opening = jnp.concatenate([values[:1], values[:1]], axis=0)
    earlier = jnp.where(lax.axis_index("ta") == 0, opening, earlier)
    return jnp.concatenate([earlier, values], axis=0)


def bordered_one(values):
    return padded_2(values, (("ha", 1), ("wa", 2)), 1)


def per_device(
    latents,
    norm1_gain,
    norm1_shift,
    up_weight,
    norm2_gain,
    norm2_shift,
    conv_a,
    norm3_gain,
    norm3_shift,
    conv_b,
):
    frames, height, across, channels = latents.shape
    latent_f = latents.astype(jnp.float32)
    activated = activate(latent_f, latent_f, norm1_gain, norm1_shift)
    spilled = spread_taps(activated, up_weight)
    from_below = passed_along(spilled[:, 0], "ha", -1)
    row_fixed = spilled[:, 1 : 2 * height + 1]
    row_fixed = jnp.concatenate(
        [row_fixed[:, :-1], row_fixed[:, -1:] + from_below[:, None]], axis=1
    )
    beside = passed_along(row_fixed[:, :, 0], "wa", -1)
    lifted = jnp.concatenate(
        [
            row_fixed[:, :, 1 : 2 * across],
            row_fixed[:, :, 2 * across : 2 * across + 1] + beside[:, :, None],
        ],
        axis=2,
    )
    lifted = lifted.astype(jnp.bfloat16)
    lifted_f = lifted.astype(jnp.float32)
    first_act = activate(lifted_f, lifted_f, norm2_gain, norm2_shift)
    out_h = 2 * height
    out_w = 2 * across
    hidden = valid_conv(
        bordered_one(causal_extend(first_act)), conv_a, frames, out_h, out_w
    ).astype(jnp.bfloat16)
    hidden_f = hidden.astype(jnp.float32)
    second_act = activate(hidden_f, hidden_f, norm3_gain, norm3_shift)
    framed = bordered_one(causal_extend(second_act))
    branch = valid_conv(framed, conv_b, frames, out_h, out_w)
    return (lifted_f + branch).astype(jnp.bfloat16)


def solution(mesh):
    return jax.shard_map(
        per_device,
        mesh=mesh,
        in_specs=(
            P(("videos", "ta"), "ha", "wa", None),
            P(),
            P(),
            P(),
            P(),
            P(),
            P(),
            P(),
            P(),
            P(),
        ),
        out_specs=P(("videos", "ta"), "ha", "wa", None),
        check_vma=False,
    )
```

profile of v0, /device:TPU:0, one launch (start us, length us, event | category | flops | bytes accessed | tf_op | source)
XLA Modules:
  0.0 204.1 jit_solution(1638593344820532898)
XLA Ops:
  1.4 34.9 %all-reduce.14 = (f32[32]{0:T(128)S(1)}, f32[32]{0:T(128)S(1)}) all-reduce(f32[32]{0:T(128)S(1)} %reduce_sum.77, f32[32]{0:T(128)S(1)} %reduce_sum.74), channel_id=1, replica_groups=mesh['videos'=2,'ha'=4,'wa'=2,'ta'=2] {'ha','wa','ta'}, use_global_device_ids=true, to_apply=%region_5.6 | all-reduce | flops 64 | bytes 512 | tf_op jit(solution)/shard_map/psum | solution.py:40
  50.9 1.3 collective-permute-start
  52.6 6.2 %collective-permute-done = f32[3,66,256]{2,1,0:T(8,128)S(1)} collective-permute-done((f32[3,66,256]{2,1,0:T(8,128)S(1)}, f32[3,66,256]{2,1,0:T(8,128)S(1)}, u32[]{:S(2)}, u32[]{:S(2)}) %collective-permute-start) | collective-permute-done | bytes 202784 | tf_op jit(solution)/shard_map/ppermute | solution.py:13
  59.0 1.3 collective-permute-start.1
  60.7 3.9 %collective-permute-done.1 = f32[3,4,256]{2,1,0:T(4,128)S(1)} collective-permute-done((f32[3,4,256]{2,1,0:T(4,128)S(1)}, f32[3,4,256]{2,1,0:T(4,128)S(1)}, u32[]{:S(2)}, u32[]{:S(2)}) %collective-permute-start.1) | collective-permute-done | bytes 12320 | tf_op jit(solution)/shard_map/ppermute | solution.py:13
  65.5 29.5 %all-reduce.13 = (f32[32]{0:T(128)S(1)}, f32[32]{0:T(128)S(1)}) all-reduce(f32[32]{0:T(128)S(1)} %reduce_sum.89, f32[32]{0:T(128)S(1)} %reduce_sum.83), channel_id=1, replica_groups=mesh['videos'=2,'ha'=4,'wa'=2,'ta'=2] {'ha','wa','ta'}, use_global_device_ids=true, to_apply=%region_11.12 | all-reduce | flops 64 | bytes 512 | tf_op jit(solution)/shard_map/psum | solution.py:40
  96.0 1.8 collective-permute-start.2
  100.0 1.3 collective-permute-start.4
  101.3 4.6 %collective-permute-start.3 = (bf16[5,1,64,256]{3,1,2,0:T(2,128)(2,1)S(1)}, bf16[5,1,64,256]{3,1,2,0:T(2,128)(2,1)S(1)}, u32[]{:S(2)}, u32[]{:S(2)}) collective-permute-start(bf16[5,1,64,256]{3,1,2,0:T(2,128)(2,1)S(1)} %get-tuple-element.81), channel_id=1, source_target_pairs={{0,4},{4,8},{8,12},{1,5},{5,9},{9,13},{2,6},{6,10},{10,14},{3,7},{... | collective-permute-start | bytes 491528 | tf_op jit(solution)/shard_map/ppermute | solution.py:23
  105.9 5.9 %collective-permute-done.4 = bf16[5,1,64,256]{3,1,2,0:T(2,128)(2,1)S(1)} collective-permute-done((bf16[5,1,64,256]{3,1,2,0:T(2,128)(2,1)S(1)}, bf16[5,1,64,256]{3,1,2,0:T(2,128)(2,1)S(1)}, u32[]{:S(2)}, u32[]{:S(2)}) %collective-permute-start.4) | collective-permute-done | bytes 163872 | tf_op jit(solution)/shard_map/ppermute | solution.py:24
  114.4 1.5 collective-permute-start.6
  117.2 1.7 pad_maximum_fusion.15
  120.1 2.3 %maximum_maximum_fusion = (bf16[5,6,65,256]{3,1,2,0:T(8,128)(2,1)S(1)}, bf16[5,6,65,256]{3,1,2,0:T(8,128)(2,1)S(1)}) fusion(bf16[5,1,64,256]{3,1,2,0:T(2,128)(2,1)S(1)} %collective-permute-done.4, bf16[3,4,64,256]{3,1,2,0:T(4,128)(2,1)S(1)} %fusion.13, bf16[2,4,64,256]{3,1,2,0:T(4,128)(2,1)S(1)} %maximum_select_fusion, ...), kind=kLoop, calls=%fused_computation.5 | loop fusion | flops 9984000 | bytes 3010560 | tf_op jit(solution)/shard_map/concatenate | solution.py:25
  122.4 1.6 fusion.182
  124.0 1.3 fusion.183
  133.7 30.7 %all-reduce.12 = (f32[32]{0:T(128)S(1)}, f32[32]{0:T(128)S(1)}) all-reduce(f32[32]{0:T(128)S(1)} %reduce_sum.113, f32[32]{0:T(128)S(1)} %reduce_sum.110), channel_id=1, replica_groups=mesh['videos'=2,'ha'=4,'wa'=2,'ta'=2] {'ha','wa','ta'}, use_global_device_ids=true, to_apply=%region_17.18 | all-reduce | flops 64 | bytes 512 | tf_op jit(solution)/shard_map/psum | solution.py:40
  165.6 1.8 collective-permute-start.7
  169.4 1.3 collective-permute-start.9
  170.7 4.6 %collective-permute-start.8 = (bf16[5,1,64,256]{3,1,2,0:T(2,128)(2,1)S(1)}, bf16[5,1,64,256]{3,1,2,0:T(2,128)(2,1)S(1)}, u32[]{:S(2)}, u32[]{:S(2)}) collective-permute-start(bf16[5,1,64,256]{3,1,2,0:T(2,128)(2,1)S(1)} %get-tuple-element.77), channel_id=1, source_target_pairs={{0,4},{4,8},{8,12},{1,5},{5,9},{9,13},{2,6},{6,10},{10,14},{3,7},{... | collective-permute-start | bytes 491528 | tf_op jit(solution)/shard_map/ppermute | solution.py:23
  175.3 6.0 %collective-permute-done.9 = bf16[5,1,64,256]{3,1,2,0:T(2,128)(2,1)S(1)} collective-permute-done((bf16[5,1,64,256]{3,1,2,0:T(2,128)(2,1)S(1)}, bf16[5,1,64,256]{3,1,2,0:T(2,128)(2,1)S(1)}, u32[]{:S(2)}, u32[]{:S(2)}) %collective-permute-start.9) | collective-permute-done | bytes 163872 | tf_op jit(solution)/shard_map/ppermute | solution.py:24
  183.8 1.3 collective-permute-start.11
  186.4 1.7 pad_maximum_fusion.6
  189.5 2.3 %maximum_maximum_fusion.1 = (bf16[5,6,65,256]{3,1,2,0:T(8,128)(2,1)S(1)}, bf16[5,6,65,256]{3,1,2,0:T(8,128)(2,1)S(1)}) fusion(bf16[5,1,64,256]{3,1,2,0:T(2,128)(2,1)S(1)} %collective-permute-done.9, bf16[3,4,64,256]{3,1,2,0:T(4,128)(2,1)S(1)} %fusion.14, bf16[2,4,64,256]{3,1,2,0:T(4,128)(2,1)S(1)} %maximum_select_fusion.1, ...), kind=kLoop, calls=%fused_computation.7 | loop fusion | flops 9984000 | bytes 3010560 | tf_op jit(solution)/shard_map/concatenate | solution.py:25
  191.8 1.6 fusion.180
  (205 shorter events, 52.3 us)
Async XLA Ops:
  50.9 44.4 %copy-start.2 = (f32[256]{0:T(256)S(1)}, f32[256]{0:T(256)}, u32[]{:S(2)}) copy-start(f32[256]{0:T(256)} %param.15) | copy-start | bytes 3076
  50.9 44.4 %copy-start.3 = (f32[256]{0:T(256)S(1)}, f32[256]{0:T(256)}, u32[]{:S(2)}) copy-start(f32[256]{0:T(256)} %param.14) | copy-start | bytes 3076
  50.9 7.8 %collective-permute-start = (f32[3,66,256]{2,1,0:T(8,128)S(1)}, f32[3,66,256]{2,1,0:T(8,128)S(1)}, u32[]{:S(2)}, u32[]{:S(2)}) collective-permute-start(f32[3,66,256]{2,1,0:T(8,128)S(1)} %get-tuple-element.53), channel_id=1, source_target_pairs={{4,0},{8,4},{12,8},{5,1},{9,5},{13,9},{6,2},{10,6},{14,10},{7,3},{... | collective-permute-start | bytes 608264 | tf_op jit(solution)/shard_map/ppermute | solution.py:13
  59.0 5.6 %collective-permute-start.1 = (f32[3,4,256]{2,1,0:T(4,128)S(1)}, f32[3,4,256]{2,1,0:T(4,128)S(1)}, u32[]{:S(2)}, u32[]{:S(2)}) collective-permute-start(f32[3,4,256]{2,1,0:T(4,128)S(1)} %fusion.176), channel_id=1, source_target_pairs={{2,0},{3,1},{6,4},{7,5},{10,8},{11,9},{14,12},{15,13},{18,16},{19,... | collective-permute-start | bytes 36872 | tf_op jit(solution)/shard_map/ppermute | solution.py:13
  96.0 2.9 %collective-permute-start.2 = (bf16[2,4,64,256]{3,1,2,0:T(4,128)(2,1)S(1)}, bf16[2,4,64,256]{3,1,2,0:T(4,128)(2,1)S(1)}, u32[]{:S(2)}, u32[]{:S(2)}) collective-permute-start(bf16[2,4,64,256]{3,1,2,0:T(4,128)(2,1)S(1)} %slice.594), channel_id=1, source_target_pairs={{0,1},{2,3},{4,5},{6,7},{8,9},{10,11},{12,13},{14,15},{16,17},{18,... | collective-permute-start | bytes 786440 | tf_op jit(solution)/shard_map/ppermute | solution.py:13
  97.9 19.0 %copy-start = (bf16[3,3,3,256,256]{4,3,2,1,0:T(8,128)(2,1)S(1)}, bf16[3,3,3,256,256]{4,3,2,1,0:T(8,128)(2,1)}, u32[]{:S(2)}) copy-start(bf16[3,3,3,256,256]{4,3,2,1,0:T(8,128)(2,1)} %param.16) | copy-start | bytes 10616836
  100.0 11.9 %collective-permute-start.4 = (bf16[5,1,64,256]{3,1,2,0:T(2,128)(2,1)S(1)}, bf16[5,1,64,256]{3,1,2,0:T(2,128)(2,1)S(1)}, u32[]{:S(2)}, u32[]{:S(2)}) collective-permute-start(bf16[5,1,64,256]{3,1,2,0:T(2,128)(2,1)S(1)} %get-tuple-element.82), channel_id=1, source_target_pairs={{4,0},{8,4},{12,8},{5,1},{9,5},{13,9},{6,2},{10,6},{14,10},{7,3},{... | collective-permute-start | bytes 491528 | tf_op jit(solution)/shard_map/ppermute | solution.py:24
  101.3 11.8 %collective-permute-start.3 = (bf16[5,1,64,256]{3,1,2,0:T(2,128)(2,1)S(1)}, bf16[5,1,64,256]{3,1,2,0:T(2,128)(2,1)S(1)}, u32[]{:S(2)}, u32[]{:S(2)}) collective-permute-start(bf16[5,1,64,256]{3,1,2,0:T(2,128)(2,1)S(1)} %get-tuple-element.81), channel_id=1, source_target_pairs={{0,4},{4,8},{8,12},{1,5},{5,9},{9,13},{2,6},{6,10},{10,14},{3,7},{... | collective-permute-start | bytes 491528 | tf_op jit(solution)/shard_map/ppermute | solution.py:23
  113.1 6.2 %collective-permute-start.5 = (bf16[5,6,1,256]{3,1,2,0:T(8,128)(2,1)S(1)}, bf16[5,6,1,256]{3,1,2,0:T(8,128)(2,1)S(1)}, u32[]{:S(2)}, u32[]{:S(2)}) collective-permute-start(bf16[5,6,1,256]{3,1,2,0:T(8,128)(2,1)S(1)} %get-tuple-element.61), channel_id=1, source_target_pairs={{0,2},{1,3},{4,6},{5,7},{8,10},{9,11},{12,14},{13,15},{16,18},{17,... | collective-permute-start | bytes 46088 | tf_op jit(solution)/shard_map/ppermute | solution.py:23
  114.4 5.7 %collective-permute-start.6 = (bf16[5,6,1,256]{3,1,2,0:T(8,128)(2,1)S(1)}, bf16[5,6,1,256]{3,1,2,0:T(8,128)(2,1)S(1)}, u32[]{:S(2)}, u32[]{:S(2)}) collective-permute-start(bf16[5,6,1,256]{3,1,2,0:T(8,128)(2,1)S(1)} %get-tuple-element.62), channel_id=1, source_target_pairs={{2,0},{3,1},{6,4},{7,5},{10,8},{11,9},{14,12},{15,13},{18,16},{19,... | collective-permute-start | bytes 46088 | tf_op jit(solution)/shard_map/ppermute | solution.py:24
  132.4 32.4 %copy-start.4 = (f32[256]{0:T(256)S(1)}, f32[256]{0:T(256)}, u32[]{:S(2)}) copy-start(f32[256]{0:T(256)} %param.18) | copy-start | bytes 3076
  132.4 32.4 %copy-start.5 = (f32[256]{0:T(256)S(1)}, f32[256]{0:T(256)}, u32[]{:S(2)}) copy-start(f32[256]{0:T(256)} %param.17) | copy-start | bytes 3076
  165.5 20.6 %copy-start.1 = (bf16[3,3,3,256,256]{4,3,2,1,0:T(8,128)(2,1)S(1)}, bf16[3,3,3,256,256]{4,3,2,1,0:T(8,128)(2,1)}, u32[]{:S(2)}) copy-start(bf16[3,3,3,256,256]{4,3,2,1,0:T(8,128)(2,1)} %param.19) | copy-start | bytes 10616836
  165.6 2.7 %collective-permute-start.7 = (bf16[2,4,64,256]{3,1,2,0:T(4,128)(2,1)S(1)}, bf16[2,4,64,256]{3,1,2,0:T(4,128)(2,1)S(1)}, u32[]{:S(2)}, u32[]{:S(2)}) collective-permute-start(bf16[2,4,64,256]{3,1,2,0:T(4,128)(2,1)S(1)} %slice.620), channel_id=1, source_target_pairs={{0,1},{2,3},{4,5},{6,7},{8,9},{10,11},{12,13},{14,15},{16,17},{18,... | collective-permute-start | bytes 786440 | tf_op jit(solution)/shard_map/ppermute | solution.py:13
  169.4 11.9 %collective-permute-start.9 = (bf16[5,1,64,256]{3,1,2,0:T(2,128)(2,1)S(1)}, bf16[5,1,64,256]{3,1,2,0:T(2,128)(2,1)S(1)}, u32[]{:S(2)}, u32[]{:S(2)}) collective-permute-start(bf16[5,1,64,256]{3,1,2,0:T(2,128)(2,1)S(1)} %get-tuple-element.78), channel_id=1, source_target_pairs={{4,0},{8,4},{12,8},{5,1},{9,5},{13,9},{6,2},{10,6},{14,10},{7,3},{... | collective-permute-start | bytes 491528 | tf_op jit(solution)/shard_map/ppermute | solution.py:24
  170.7 11.8 %collective-permute-start.8 = (bf16[5,1,64,256]{3,1,2,0:T(2,128)(2,1)S(1)}, bf16[5,1,64,256]{3,1,2,0:T(2,128)(2,1)S(1)}, u32[]{:S(2)}, u32[]{:S(2)}) collective-permute-start(bf16[5,1,64,256]{3,1,2,0:T(2,128)(2,1)S(1)} %get-tuple-element.77), channel_id=1, source_target_pairs={{0,4},{4,8},{8,12},{1,5},{5,9},{9,13},{2,6},{6,10},{10,14},{3,7},{... | collective-permute-start | bytes 491528 | tf_op jit(solution)/shard_map/ppermute | solution.py:23
  182.5 6.0 %collective-permute-start.10 = (bf16[5,6,1,256]{3,1,2,0:T(8,128)(2,1)S(1)}, bf16[5,6,1,256]{3,1,2,0:T(8,128)(2,1)S(1)}, u32[]{:S(2)}, u32[]{:S(2)}) collective-permute-start(bf16[5,6,1,256]{3,1,2,0:T(8,128)(2,1)S(1)} %get-tuple-element.57), channel_id=1, source_target_pairs={{0,2},{1,3},{4,6},{5,7},{8,10},{9,11},{12,14},{13,15},{16,18},{17,... | collective-permute-start | bytes 46088 | tf_op jit(solution)/shard_map/ppermute | solution.py:23
  183.8 5.7 %collective-permute-start.11 = (bf16[5,6,1,256]{3,1,2,0:T(8,128)(2,1)S(1)}, bf16[5,6,1,256]{3,1,2,0:T(8,128)(2,1)S(1)}, u32[]{:S(2)}, u32[]{:S(2)}) collective-permute-start(bf16[5,6,1,256]{3,1,2,0:T(8,128)(2,1)S(1)} %get-tuple-element.58), channel_id=1, source_target_pairs={{2,0},{3,1},{6,4},{7,5},{10,8},{11,9},{14,12},{15,13},{18,16},{19,... | collective-permute-start | bytes 46088 | tf_op jit(solution)/shard_map/ppermute | solution.py:24
where the time goes:
time: 205 us; the launch traced here: 204 us
  blocking collectives  95.1 us (46%)
  waiting for transfers between devices  28 us (14%)
  matrix products  24.9 us (12%)
  starting transfers between devices  23.2 us (11%)
  other arithmetic  18.4 us (9%)
  local copies, waits for them, and re-layouts  13 us (6%)
    psum x3, blocking collectives, activate(): lax.psum((jnp.sum(grouped, axis=(0, 2)), jnp.sum(grouped * grouped, axis=...  95.1 us
    dot_general x54, matrix products, valid_conv(): jnp.dot(window.reshape(-1, window.shape[-1]), kernel[step_t, step_y, step...  14.4 us
    ppermute x4, waiting for transfers between devices, padded_2(): after = lax.ppermute(initial, axis, down)  13.7 us
    ppermute x4, waiting for transfers between devices, passed_along(): return lax.ppermute(block, axis, route)  12 us
    ppermute x4, starting transfers between devices, padded_2(): before = lax.ppermute(last, axis, up)  11.7 us
    concatenate x6, other arithmetic, padded_2(): x = jnp.concatenate([before, x, after], axis=dim)  10.1 us
    slice x56, local copies, waits for them, and re-layouts, valid_conv(): padded[step_t:step_t + frames, step_y:step_y + height, step_x:step_x + ac...  8.07 us
    dot_general x6, matrix products, spread_taps(): jnp.dot(flattened, kernel[tap_y, tap_x], preferred_element_type=jnp.float32)  6.97 us
  transfers between devices with their start and end apart: 12, of which 10 were waited for; matrix products, arithmetic and copies ran while one was open for 4% of the time, Pallas kernels for 0%

commit v1 on v0

--- a/solution.py
+++ b/solution.py
@@ -38,7 +38,10 @@
         * lax.axis_size("ta")
     )
     totals, squares = lax.psum(
-        (jnp.sum(grouped, axis=(0, 2)), jnp.sum(grouped * grouped, axis=(0, 2))), ("ha", "wa", "ta")
+        lax.psum(
+            (jnp.sum(grouped, axis=(0, 2)), jnp.sum(grouped * grouped, axis=(0, 2))), ("wa", "ta")
+        ),
+        "ha",
     )
     average = totals / entries
     spread = squares / entries - average * average

time: 205 us -> 164 us (0.80)
  blocking collectives: 95.1 us -> 52.3 us
  starting transfers between devices: 23.2 us -> 25.3 us
    psum x3, blocking collectives: 95.1 us -> 20.2 us  [activate(): lax.psum((jnp.sum(grouped, axis=(0, 2)), jnp.sum(grouped * grouped, axis=...]
    psum x0 -> x3, blocking collectives: none -> 32.1 us  [activate(): lax.psum(lax.psum((jnp.sum(grouped, axis=(0, 2)), jnp.sum(grouped * group...]
    ppermute x4, starting transfers between devices: 11.7 us -> 14.3 us  [padded_2(): before = lax.ppermute(last, axis, up)]
  transfers between devices with their start and end apart: 12 -> 12, of which waited for: 10 -> 10; matrix products, arithmetic and copies ran while one was open for 4% -> 5% of each run, Pallas kernels for 0% -> 0%
where the time goes in v1:
time: 164 us
  blocking collectives  52.3 us (32%)
  waiting for transfers between devices  28.2 us (17%)
  starting transfers between devices  25.3 us (15%)
  matrix products  24.9 us (15%)
  other arithmetic  18.4 us (11%)
  local copies, waits for them, and re-layouts  13 us (8%)
    psum x3, blocking collectives, activate(): lax.psum(lax.psum((jnp.sum(grouped, axis=(0, 2)), jnp.sum(grouped * group...  32.1 us
    psum x3, blocking collectives, activate(): lax.psum((jnp.sum(grouped, axis=(0, 2)), jnp.sum(grouped * grouped, axis=...  20.2 us
    dot_general x54, matrix products, valid_conv(): jnp.dot(window.reshape(-1, window.shape[-1]), kernel[step_t, step_y, step...  14.4 us
    ppermute x4, starting transfers between devices, padded_2(): before = lax.ppermute(last, axis, up)  14.3 us
    ppermute x4, waiting for transfers between devices, padded_2(): after = lax.ppermute(initial, axis, down)  13.9 us
    ppermute x4, waiting for transfers between devices, passed_along(): return lax.ppermute(block, axis, route)  12 us
    concatenate x6, other arithmetic, padded_2(): x = jnp.concatenate([before, x, after], axis=dim)  10.1 us
    slice x56, local copies, waits for them, and re-layouts, valid_conv(): padded[step_t:step_t + frames, step_y:step_y + height, step_x:step_x + ac...  8.07 us
  transfers between devices with their start and end apart: 12, of which 10 were waited for; matrix products, arithmetic and copies ran while one was open for 5% of the time, Pallas kernels for 0%

profile of v1, /device:TPU:0, one launch (start us, length us, event | category | flops | bytes accessed | tf_op | source)
XLA Modules:
  0.0 163.6 jit_solution(10308665977755901057)
XLA Ops:
  1.4 8.3 %all-reduce.14 = (f32[32]{0:T(128)S(1)}, f32[32]{0:T(128)S(1)}) all-reduce(f32[32]{0:T(128)S(1)} %reduce_sum.77, f32[32]{0:T(128)S(1)} %reduce_sum.74), channel_id=1, replica_groups=mesh['videos'=2,'ha'=4,'wa'=2,'ta'=2] {'wa','ta'}, use_global_device_ids=true, to_apply=%region_6.7 | all-reduce | flops 64 | bytes 512 | tf_op jit(solution)/shard_map/psum | solution.py:41
  9.7 11.9 %all-reduce.17 = (f32[32]{0:T(128)S(1)}, f32[32]{0:T(128)S(1)}) all-reduce(f32[32]{0:T(128)S(1)} %get-tuple-element.15, f32[32]{0:T(128)S(1)} %get-tuple-element.16), channel_id=1, replica_groups=mesh['videos'=2,'ha'=4,'wa'=2,'ta'=2] {'ha'}, use_global_device_ids=true, to_apply=%region_7.8 | all-reduce | flops 64 | bytes 512 | tf_op jit(solution)/shard_map/psum | solution.py:40
  38.0 6.2 %collective-permute-done = f32[3,66,256]{2,1,0:T(8,128)S(1)} collective-permute-done((f32[3,66,256]{2,1,0:T(8,128)S(1)}, f32[3,66,256]{2,1,0:T(8,128)S(1)}, u32[]{:S(2)}, u32[]{:S(2)}) %collective-permute-start) | collective-permute-done | bytes 202784 | tf_op jit(solution)/shard_map/ppermute | solution.py:13
  46.1 3.9 %collective-permute-done.1 = f32[3,4,256]{2,1,0:T(4,128)S(1)} collective-permute-done((f32[3,4,256]{2,1,0:T(4,128)S(1)}, f32[3,4,256]{2,1,0:T(4,128)S(1)}, u32[]{:S(2)}, u32[]{:S(2)}) %collective-permute-start.1) | collective-permute-done | bytes 12320 | tf_op jit(solution)/shard_map/ppermute | solution.py:13
  50.9 5.8 %all-reduce.13 = (f32[32]{0:T(128)S(1)}, f32[32]{0:T(128)S(1)}) all-reduce(f32[32]{0:T(128)S(1)} %reduce_sum.89, f32[32]{0:T(128)S(1)} %reduce_sum.83), channel_id=1, replica_groups=mesh['videos'=2,'ha'=4,'wa'=2,'ta'=2] {'wa','ta'}, use_global_device_ids=true, to_apply=%region_14.15 | all-reduce | flops 64 | bytes 512 | tf_op jit(solution)/shard_map/psum | solution.py:41
  56.6 8.4 %all-reduce.16 = (f32[32]{0:T(128)S(1)}, f32[32]{0:T(128)S(1)}) all-reduce(f32[32]{0:T(128)S(1)} %get-tuple-element.13, f32[32]{0:T(128)S(1)} %get-tuple-element.14), channel_id=1, replica_groups=mesh['videos'=2,'ha'=4,'wa'=2,'ta'=2] {'ha'}, use_global_device_ids=true, to_apply=%region_15.16 | all-reduce | flops 64 | bytes 512 | tf_op jit(solution)/shard_map/psum | solution.py:40
  66.1 1.3 collective-permute-start.2
  70.8 4.6 %collective-permute-start.3 = (bf16[5,1,64,256]{3,1,2,0:T(2,128)(2,1)S(1)}, bf16[5,1,64,256]{3,1,2,0:T(2,128)(2,1)S(1)}, u32[]{:S(2)}, u32[]{:S(2)}) collective-permute-start(bf16[5,1,64,256]{3,1,2,0:T(2,128)(2,1)S(1)} %get-tuple-element.87), channel_id=1, source_target_pairs={{0,4},{4,8},{8,12},{1,5},{5,9},{9,13},{2,6},{6,10},{10,14},{3,7},{... | collective-permute-start | bytes 491528 | tf_op jit(solution)/shard_map/ppermute | solution.py:23
  75.5 6.2 %collective-permute-done.4 = bf16[5,1,64,256]{3,1,2,0:T(2,128)(2,1)S(1)} collective-permute-done((bf16[5,1,64,256]{3,1,2,0:T(2,128)(2,1)S(1)}, bf16[5,1,64,256]{3,1,2,0:T(2,128)(2,1)S(1)}, u32[]{:S(2)}, u32[]{:S(2)}) %collective-permute-start.4) | collective-permute-done | bytes 163872 | tf_op jit(solution)/shard_map/ppermute | solution.py:24
  82.9 1.7 %collective-permute-start.5 = (bf16[5,6,1,256]{3,1,2,0:T(8,128)(2,1)S(1)}, bf16[5,6,1,256]{3,1,2,0:T(8,128)(2,1)S(1)}, u32[]{:S(2)}, u32[]{:S(2)}) collective-permute-start(bf16[5,6,1,256]{3,1,2,0:T(8,128)(2,1)S(1)} %get-tuple-element.67), channel_id=1, source_target_pairs={{0,2},{1,3},{4,6},{5,7},{8,10},{9,11},{12,14},{13,15},{16,18},{17,... | collective-permute-start | bytes 46088 | tf_op jit(solution)/shard_map/ppermute | solution.py:23
  84.6 1.5 collective-permute-start.6
  87.4 1.7 %pad_maximum_fusion.15 = (bf16[3,4,64,256]{3,1,2,0:T(4,128)(2,1)S(1)}, bf16[3,4,64,256]{3,1,2,0:T(4,128)(2,1)S(1)}, bf16[3,4,64,256]{3,1,2,0:T(4,128)(2,1)S(1)},...) fusion(bf16[5,1,64,256]{3,1,2,0:T(2,128)(2,1)S(1)} %collective-permute-done.4, ...), kind=kLoop, calls=%fused_computation.128 | loop fusion | flops 5111808 | bytes 2785280 | tf_op jit(solution)/shard_map/concatenate | solution.py:25
  90.3 2.3 %maximum_maximum_fusion = (bf16[5,6,65,256]{3,1,2,0:T(8,128)(2,1)S(1)}, bf16[5,6,65,256]{3,1,2,0:T(8,128)(2,1)S(1)}) fusion(bf16[5,1,64,256]{3,1,2,0:T(2,128)(2,1)S(1)} %collective-permute-done.4, bf16[3,4,64,256]{3,1,2,0:T(4,128)(2,1)S(1)} %fusion.13, bf16[2,4,64,256]{3,1,2,0:T(4,128)(2,1)S(1)} %maximum_select_fusion, ...), kind=kLoop, calls=%fused_computation.5 | loop fusion | flops 9984000 | bytes 3010560 | tf_op jit(solution)/shard_map/concatenate | solution.py:25
  92.6 1.6 fusion.182
  94.2 1.3 fusion.183
  103.9 6.1 %all-reduce.12 = (f32[32]{0:T(128)S(1)}, f32[32]{0:T(128)S(1)}) all-reduce(f32[32]{0:T(128)S(1)} %reduce_sum.113, f32[32]{0:T(128)S(1)} %reduce_sum.110), channel_id=1, replica_groups=mesh['videos'=2,'ha'=4,'wa'=2,'ta'=2] {'wa','ta'}, use_global_device_ids=true, to_apply=%region_22.23 | all-reduce | flops 64 | bytes 512 | tf_op jit(solution)/shard_map/psum | solution.py:41
  110.0 11.8 %all-reduce.15 = (f32[32]{0:T(128)S(1)}, f32[32]{0:T(128)S(1)}) all-reduce(f32[32]{0:T(128)S(1)} %get-tuple-element.11, f32[32]{0:T(128)S(1)} %get-tuple-element.12), channel_id=1, replica_groups=mesh['videos'=2,'ha'=4,'wa'=2,'ta'=2] {'ha'}, use_global_device_ids=true, to_apply=%region_23.24 | all-reduce | flops 64 | bytes 512 | tf_op jit(solution)/shard_map/psum | solution.py:40
  123.0 1.8 %collective-permute-start.7 = (bf16[2,4,64,256]{3,1,2,0:T(4,128)(2,1)S(1)}, bf16[2,4,64,256]{3,1,2,0:T(4,128)(2,1)S(1)}, u32[]{:S(2)}, u32[]{:S(2)}) collective-permute-start(bf16[2,4,64,256]{3,1,2,0:T(4,128)(2,1)S(1)} %slice.620), channel_id=1, source_target_pairs={{0,1},{2,3},{4,5},{6,7},{8,9},{10,11},{12,13},{14,15},{16,17},{18,... | collective-permute-start | bytes 786440 | tf_op jit(solution)/shard_map/ppermute | solution.py:13
  128.0 4.6 %collective-permute-start.8 = (bf16[5,1,64,256]{3,1,2,0:T(2,128)(2,1)S(1)}, bf16[5,1,64,256]{3,1,2,0:T(2,128)(2,1)S(1)}, u32[]{:S(2)}, u32[]{:S(2)}) collective-permute-start(bf16[5,1,64,256]{3,1,2,0:T(2,128)(2,1)S(1)} %get-tuple-element.83), channel_id=1, source_target_pairs={{0,4},{4,8},{8,12},{1,5},{5,9},{9,13},{2,6},{6,10},{10,14},{3,7},{... | collective-permute-start | bytes 491528 | tf_op jit(solution)/shard_map/ppermute | solution.py:23
  132.6 6.0 %collective-permute-done.9 = bf16[5,1,64,256]{3,1,2,0:T(2,128)(2,1)S(1)} collective-permute-done((bf16[5,1,64,256]{3,1,2,0:T(2,128)(2,1)S(1)}, bf16[5,1,64,256]{3,1,2,0:T(2,128)(2,1)S(1)}, u32[]{:S(2)}, u32[]{:S(2)}) %collective-permute-start.9) | collective-permute-done | bytes 163872 | tf_op jit(solution)/shard_map/ppermute | solution.py:24
  139.8 3.4 %collective-permute-start.10 = (bf16[5,6,1,256]{3,1,2,0:T(8,128)(2,1)S(1)}, bf16[5,6,1,256]{3,1,2,0:T(8,128)(2,1)S(1)}, u32[]{:S(2)}, u32[]{:S(2)}) collective-permute-start(bf16[5,6,1,256]{3,1,2,0:T(8,128)(2,1)S(1)} %get-tuple-element.63), channel_id=1, source_target_pairs={{0,2},{1,3},{4,6},{5,7},{8,10},{9,11},{12,14},{13,15},{16,18},{17,... | collective-permute-start | bytes 46088 | tf_op jit(solution)/shard_map/ppermute | solution.py:23
  145.8 1.7 %pad_maximum_fusion.6 = (bf16[3,4,64,256]{3,1,2,0:T(4,128)(2,1)S(1)}, bf16[3,4,64,256]{3,1,2,0:T(4,128)(2,1)S(1)}, bf16[3,4,64,256]{3,1,2,0:T(4,128)(2,1)S(1)}, ...) fusion(bf16[5,1,64,256]{3,1,2,0:T(2,128)(2,1)S(1)} %collective-permute-done.9, ...), kind=kLoop, calls=%fused_computation.119 | loop fusion | flops 5111808 | bytes 2785280 | tf_op jit(solution)/shard_map/concatenate | solution.py:25
  148.9 2.3 %maximum_maximum_fusion.1 = (bf16[5,6,65,256]{3,1,2,0:T(8,128)(2,1)S(1)}, bf16[5,6,65,256]{3,1,2,0:T(8,128)(2,1)S(1)}) fusion(bf16[5,1,64,256]{3,1,2,0:T(2,128)(2,1)S(1)} %collective-permute-done.9, bf16[3,4,64,256]{3,1,2,0:T(4,128)(2,1)S(1)} %fusion.14, bf16[2,4,64,256]{3,1,2,0:T(4,128)(2,1)S(1)} %maximum_select_fusion.1, ...), kind=kLoop, calls=%fused_computation.7 | loop fusion | flops 9984000 | bytes 3010560 | tf_op jit(solution)/shard_map/concatenate | solution.py:25
  151.3 1.6 fusion.180
  (208 shorter events, 56.2 us)
Async XLA Ops:
  36.3 29.1 %copy-start.2 = (f32[256]{0:T(256)S(1)}, f32[256]{0:T(256)}, u32[]{:S(2)}) copy-start(f32[256]{0:T(256)} %param.15) | copy-start | bytes 3076
  36.3 29.1 %copy-start.3 = (f32[256]{0:T(256)S(1)}, f32[256]{0:T(256)}, u32[]{:S(2)}) copy-start(f32[256]{0:T(256)} %param.14) | copy-start | bytes 3076
  36.3 7.8 %collective-permute-start = (f32[3,66,256]{2,1,0:T(8,128)S(1)}, f32[3,66,256]{2,1,0:T(8,128)S(1)}, u32[]{:S(2)}, u32[]{:S(2)}) collective-permute-start(f32[3,66,256]{2,1,0:T(8,128)S(1)} %get-tuple-element.59), channel_id=1, source_target_pairs={{4,0},{8,4},{12,8},{5,1},{9,5},{13,9},{6,2},{10,6},{14,10},{7,3},{... | collective-permute-start | bytes 608264 | tf_op jit(solution)/shard_map/ppermute | solution.py:13
  44.4 5.6 %collective-permute-start.1 = (f32[3,4,256]{2,1,0:T(4,128)S(1)}, f32[3,4,256]{2,1,0:T(4,128)S(1)}, u32[]{:S(2)}, u32[]{:S(2)}) collective-permute-start(f32[3,4,256]{2,1,0:T(4,128)S(1)} %fusion.176), channel_id=1, source_target_pairs={{2,0},{3,1},{6,4},{7,5},{10,8},{11,9},{14,12},{15,13},{18,16},{19,... | collective-permute-start | bytes 36872 | tf_op jit(solution)/shard_map/ppermute | solution.py:13
  66.1 2.4 %collective-permute-start.2 = (bf16[2,4,64,256]{3,1,2,0:T(4,128)(2,1)S(1)}, bf16[2,4,64,256]{3,1,2,0:T(4,128)(2,1)S(1)}, u32[]{:S(2)}, u32[]{:S(2)}) collective-permute-start(bf16[2,4,64,256]{3,1,2,0:T(4,128)(2,1)S(1)} %slice.594), channel_id=1, source_target_pairs={{0,1},{2,3},{4,5},{6,7},{8,9},{10,11},{12,13},{14,15},{16,17},{18,... | collective-permute-start | bytes 786440 | tf_op jit(solution)/shard_map/ppermute | solution.py:13
  67.4 19.6 %copy-start = (bf16[3,3,3,256,256]{4,3,2,1,0:T(8,128)(2,1)S(1)}, bf16[3,3,3,256,256]{4,3,2,1,0:T(8,128)(2,1)}, u32[]{:S(2)}) copy-start(bf16[3,3,3,256,256]{4,3,2,1,0:T(8,128)(2,1)} %param.16) | copy-start | bytes 10616836
  69.5 12.1 %collective-permute-start.4 = (bf16[5,1,64,256]{3,1,2,0:T(2,128)(2,1)S(1)}, bf16[5,1,64,256]{3,1,2,0:T(2,128)(2,1)S(1)}, u32[]{:S(2)}, u32[]{:S(2)}) collective-permute-start(bf16[5,1,64,256]{3,1,2,0:T(2,128)(2,1)S(1)} %get-tuple-element.88), channel_id=1, source_target_pairs={{4,0},{8,4},{12,8},{5,1},{9,5},{13,9},{6,2},{10,6},{14,10},{7,3},{... | collective-permute-start | bytes 491528 | tf_op jit(solution)/shard_map/ppermute | solution.py:24
  70.8 12.0 %collective-permute-start.3 = (bf16[5,1,64,256]{3,1,2,0:T(2,128)(2,1)S(1)}, bf16[5,1,64,256]{3,1,2,0:T(2,128)(2,1)S(1)}, u32[]{:S(2)}, u32[]{:S(2)}) collective-permute-start(bf16[5,1,64,256]{3,1,2,0:T(2,128)(2,1)S(1)} %get-tuple-element.87), channel_id=1, source_target_pairs={{0,4},{4,8},{8,12},{1,5},{5,9},{9,13},{2,6},{6,10},{10,14},{3,7},{... | collective-permute-start | bytes 491528 | tf_op jit(solution)/shard_map/ppermute | solution.py:23
  82.9 6.6 %collective-permute-start.5 = (bf16[5,6,1,256]{3,1,2,0:T(8,128)(2,1)S(1)}, bf16[5,6,1,256]{3,1,2,0:T(8,128)(2,1)S(1)}, u32[]{:S(2)}, u32[]{:S(2)}) collective-permute-start(bf16[5,6,1,256]{3,1,2,0:T(8,128)(2,1)S(1)} %get-tuple-element.67), channel_id=1, source_target_pairs={{0,2},{1,3},{4,6},{5,7},{8,10},{9,11},{12,14},{13,15},{16,18},{17,... | collective-permute-start | bytes 46088 | tf_op jit(solution)/shard_map/ppermute | solution.py:23
  84.6 5.7 %collective-permute-start.6 = (bf16[5,6,1,256]{3,1,2,0:T(8,128)(2,1)S(1)}, bf16[5,6,1,256]{3,1,2,0:T(8,128)(2,1)S(1)}, u32[]{:S(2)}, u32[]{:S(2)}) collective-permute-start(bf16[5,6,1,256]{3,1,2,0:T(8,128)(2,1)S(1)} %get-tuple-element.68), channel_id=1, source_target_pairs={{2,0},{3,1},{6,4},{7,5},{10,8},{11,9},{14,12},{15,13},{18,16},{19,... | collective-permute-start | bytes 46088 | tf_op jit(solution)/shard_map/ppermute | solution.py:24
  102.6 19.5 %copy-start.4 = (f32[256]{0:T(256)S(1)}, f32[256]{0:T(256)}, u32[]{:S(2)}) copy-start(f32[256]{0:T(256)} %param.18) | copy-start | bytes 3076
  102.6 19.5 %copy-start.5 = (f32[256]{0:T(256)S(1)}, f32[256]{0:T(256)}, u32[]{:S(2)}) copy-start(f32[256]{0:T(256)} %param.17) | copy-start | bytes 3076
  122.9 22.7 %copy-start.1 = (bf16[3,3,3,256,256]{4,3,2,1,0:T(8,128)(2,1)S(1)}, bf16[3,3,3,256,256]{4,3,2,1,0:T(8,128)(2,1)}, u32[]{:S(2)}) copy-start(bf16[3,3,3,256,256]{4,3,2,1,0:T(8,128)(2,1)} %param.19) | copy-start | bytes 10616836
  123.0 2.7 %collective-permute-start.7 = (bf16[2,4,64,256]{3,1,2,0:T(4,128)(2,1)S(1)}, bf16[2,4,64,256]{3,1,2,0:T(4,128)(2,1)S(1)}, u32[]{:S(2)}, u32[]{:S(2)}) collective-permute-start(bf16[2,4,64,256]{3,1,2,0:T(4,128)(2,1)S(1)} %slice.620), channel_id=1, source_target_pairs={{0,1},{2,3},{4,5},{6,7},{8,9},{10,11},{12,13},{14,15},{16,17},{18,... | collective-permute-start | bytes 786440 | tf_op jit(solution)/shard_map/ppermute | solution.py:13
  126.7 11.9 %collective-permute-start.9 = (bf16[5,1,64,256]{3,1,2,0:T(2,128)(2,1)S(1)}, bf16[5,1,64,256]{3,1,2,0:T(2,128)(2,1)S(1)}, u32[]{:S(2)}, u32[]{:S(2)}) collective-permute-start(bf16[5,1,64,256]{3,1,2,0:T(2,128)(2,1)S(1)} %get-tuple-element.84), channel_id=1, source_target_pairs={{4,0},{8,4},{12,8},{5,1},{9,5},{13,9},{6,2},{10,6},{14,10},{7,3},{... | collective-permute-start | bytes 491528 | tf_op jit(solution)/shard_map/ppermute | solution.py:24
  128.0 11.8 %collective-permute-start.8 = (bf16[5,1,64,256]{3,1,2,0:T(2,128)(2,1)S(1)}, bf16[5,1,64,256]{3,1,2,0:T(2,128)(2,1)S(1)}, u32[]{:S(2)}, u32[]{:S(2)}) collective-permute-start(bf16[5,1,64,256]{3,1,2,0:T(2,128)(2,1)S(1)} %get-tuple-element.83), channel_id=1, source_target_pairs={{0,4},{4,8},{8,12},{1,5},{5,9},{9,13},{2,6},{6,10},{10,14},{3,7},{... | collective-permute-start | bytes 491528 | tf_op jit(solution)/shard_map/ppermute | solution.py:23
  139.8 8.2 %collective-permute-start.10 = (bf16[5,6,1,256]{3,1,2,0:T(8,128)(2,1)S(1)}, bf16[5,6,1,256]{3,1,2,0:T(8,128)(2,1)S(1)}, u32[]{:S(2)}, u32[]{:S(2)}) collective-permute-start(bf16[5,6,1,256]{3,1,2,0:T(8,128)(2,1)S(1)} %get-tuple-element.63), channel_id=1, source_target_pairs={{0,2},{1,3},{4,6},{5,7},{8,10},{9,11},{12,14},{13,15},{16,18},{17,... | collective-permute-start | bytes 46088 | tf_op jit(solution)/shard_map/ppermute | solution.py:23
  143.2 5.7 %collective-permute-start.11 = (bf16[5,6,1,256]{3,1,2,0:T(8,128)(2,1)S(1)}, bf16[5,6,1,256]{3,1,2,0:T(8,128)(2,1)S(1)}, u32[]{:S(2)}, u32[]{:S(2)}) collective-permute-start(bf16[5,6,1,256]{3,1,2,0:T(8,128)(2,1)S(1)} %get-tuple-element.64), channel_id=1, source_target_pairs={{2,0},{3,1},{6,4},{7,5},{10,8},{11,9},{14,12},{15,13},{18,16},{19,... | collective-permute-start | bytes 46088 | tf_op jit(solution)/shard_map/ppermute | solution.py:24
